TPU v7x, 512 devices: a whole 4x8x8 slice. The times are simulated.
512 devices in a mesh: ctx: 64 (over y, x, core), head: 8 (over z).
Axes of the slice: x: 4, y: 8, z: 8, core: 2. Of those that a mesh axis runs over, the one named last changes fastest.
Arguments:
- tokens: bfloat16 [65536, 2048], P('ctx', 'head'), may hold values from -6 to 6
- w_qkv: bfloat16 [3, 2048, 2048], P(None, 'ctx', 'head'), may hold values from -0.125 to 0.125
- out_gain: float32 [2048], P('head'), may hold values from 0.25 to 1.75
- seg_ids: int32 [65536], P('ctx'), may hold values from 0 to 15, never falling along the last dimension, each value on 1 to 16384 neighbouring positions
Outputs:
- attended: bfloat16 [65536, 2048], P('ctx', 'head')
Inputs may be any that keep to these rules, and one draw needn't show every extreme that they name: `seg_ids`: segment numbers never fall along the stream; each segment covers 1 to 16384 consecutive tokens, and one covers exactly 16384.
All inputs are finite; a program needn't handle non-finite values.
Results may differ from a plain program's by a relative error of at most 0.012.
Values may be sent and summed in bfloat16 or wider, within the bound.
No kernel may reach another device: no remote copies, remote signals or barrier semaphores. Data moves between devices by JAX's collectives and lax.ppermute only.
A program may use at most 64 MiB of HBM per device.

v0:
```python
import jax
import jax.numpy as jnp
from jax import lax
from jax.sharding import PartitionSpec as P

HEAD_DIM = 128


def passed_along(value, axis, steps):
    count = lax.axis_size(axis)
    leading, last = (max(0, -steps), min(count, count - steps))
    return lax.ppermute(value, axis, [(source, source + steps) for source in range(leading, last)])


def feature_map(values):
    return (jax.nn.elu(values.astype(jnp.float32)) + 1.0).astype(jnp.bfloat16)


def combine(earlier, later):
    first_state, first_tail = earlier
    later_state, later_tail = later
    linked = (first_tail == later_tail) | (later_tail < 0.0)
    return (
        later_state + jnp.where(linked, first_state, 0.0),
        jnp.where(later_tail < 0.0, first_tail, later_tail),
    )


def prepare(projected, segment):
    row_count = segment.shape[0]
    head_count = projected.shape[2] // HEAD_DIM
    queries = feature_map(projected[0]).reshape(row_count, head_count, HEAD_DIM)
    key_map = feature_map(projected[1]).reshape(row_count, head_count, HEAD_DIM)
    values = projected[2].reshape(row_count, head_count, HEAD_DIM)
    seg_float = segment.astype(jnp.float32)
    tail_id = seg_float[-1]
    key_tail = jnp.where((seg_float == tail_id)[:, None, None], key_map, jnp.zeros_like(key_map))
    kv_state = jnp.einsum("thd,the->hde", key_tail, values, preferred_element_type=jnp.float32)
    return (queries, key_map, values, seg_float, kv_state, tail_id)


def complete(queries, key_map, values, seg_float, state_in, tail_in, out_gain):
    row_count, head_count = (queries.shape[0], queries.shape[1])
    state_low = state_in.astype(jnp.bfloat16)
    prefix = jnp.einsum("thd,hde->the", queries, state_low, preferred_element_type=jnp.float32)
    prefix = jnp.where((seg_float == tail_in)[:, None, None], prefix, 0.0)
    block_rows = min(512, row_count)
    positions = jnp.arange(row_count, dtype=jnp.int32)

    def one_block(blk_no):
        first_row = blk_no * block_rows
        query_blk = lax.dynamic_slice_in_dim(queries, first_row, block_rows, 0)
        query_pos = first_row + jnp.arange(block_rows, dtype=jnp.int32)
        query_seg = lax.dynamic_slice_in_dim(seg_float, first_row, block_rows, 0)
        scores = jnp.einsum("bhd,shd->hbs", query_blk, key_map, preferred_element_type=jnp.float32)
        visible = (positions[None, :] <= query_pos[:, None]) & (
            seg_float[None, :] == query_seg[:, None]
        )
        weights = jnp.where(visible[None], scores, 0.0).astype(jnp.bfloat16)
        return jnp.einsum("hbs,she->bhe", weights, values, preferred_element_type=jnp.float32)

    local_part = lax.map(one_block, jnp.arange(row_count // block_rows, dtype=jnp.int32))
    numerator = local_part.reshape(row_count, head_count, HEAD_DIM) + prefix
    inv_norm = lax.rsqrt(jnp.mean(numerator * numerator, axis=-1, keepdims=True) + 1e-05)
    result = numerator * inv_norm * out_gain.reshape(head_count, HEAD_DIM)
    return result.astype(jnp.bfloat16).reshape(row_count, head_count * HEAD_DIM)


def per_device(tokens, w_qkv, out_gain, seg_ids):
    whole = lax.all_gather(tokens, "head", axis=1, tiled=True)
    projected = jnp.einsum(
        "tr,grc->gtc",
        whole,
        lax.all_gather(w_qkv, "ctx", axis=1, tiled=True),
        preferred_element_type=jnp.float32,
    ).astype(jnp.bfloat16)
    queries, key_map, values, seg_float, kv_state, tail_id = prepare(projected, seg_ids)
    empty_state = jnp.zeros_like(kv_state)
    own_pair = (kv_state, tail_id)

    def hand_round(turn_no, carried):
        running, _ = carried
        incoming = (
            passed_along(running[0].astype(jnp.bfloat16), "ctx", 1).astype(jnp.float32),
            passed_along(running[1].astype(jnp.bfloat16), "ctx", 1).astype(jnp.float32),
        )
        return (combine(incoming, own_pair), incoming)

    start_pair = (empty_state, jnp.array(-1.0, jnp.float32))
    _, arrived = lax.fori_loop(0, lax.axis_size("ctx") - 1, hand_round, (own_pair, start_pair))
    state_in, tail_in = arrived
    return complete(queries, key_map, values, seg_float, state_in, tail_in, out_gain)


def solution(mesh):
    placed = (P("ctx", "head"), P(None, "ctx", "head"), P("head"), P("ctx"))
    return jax.shard_map(
        per_device, mesh=mesh, in_specs=placed, out_specs=P("ctx", "head"), check_vma=False
    )
```

profile of v0, /device:TPU:32, one launch (start us, length us, event | category | flops | bytes accessed | tf_op | source)
XLA Modules:
  0.0 1084.5 jit_solution(1804793181118891656)
XLA Ops:
  12.1 84.4 %all-gather.3.cloned.1.call-done = bf16[3,2048,256]{2,1,0:T(8,128)(2,1)} async-done(((bf16[3,32,256]{2,1,0:T(8,128)(2,1)}), bf16[3,2048,256]{2,1,0:T(8,128)(2,1)}) %all-gather.3.cloned.1.call-update) | async-done | bytes 3145744 | tf_op jit(solution)/shard_map/all_gather | solution.py:74
  96.5 67.6 %all-gather.5.cloned.1.call-done = bf16[1024,2048]{1,0:T(8,128)(2,1)} async-done(((bf16[1024,256]{1,0:T(8,128)(2,1)}), bf16[1024,2048]{1,0:T(8,128)(2,1)}) %all-gather.5.cloned.1.call-update) | async-done | bytes 4194320 | tf_op jit(solution)/shard_map/all_gather | solution.py:70
  164.0 6.6 fusion.15
  176.5 877.2 %while.28 = (s32[]{:T(128)}, bf16[2,128,128]{2,1,0:T(8,128)(2,1)S(1)}, bf16[]{:T(256)}, bf16[2,128,128]{2,1,0:T(8,128)(2,1)}, f32[]{:T(128)}, /*index=5*/f32[]{:...) while((s32[]{:T(128)}, bf16[2,128,128]{2,1,0:T(8,128)(2,1)S(1)}, bf16[]{:T(256)}, ...), condition=%wide.region_3.4_spmd, body=%wide.region_2.3_spmd.sunk | while | flops 163846 | bytes 590031 | solution.py:90
  195.3 5.4 collective-permute-done
  209.2 5.4 collective-permute-done
  223.1 5.4 collective-permute-done
  264.9 5.4 collective-permute-done
  278.8 5.4 collective-permute-done
  292.7 5.4 collective-permute-done
  306.6 5.4 collective-permute-done
  320.6 5.4 collective-permute-done
  334.5 5.4 collective-permute-done
  348.4 5.4 collective-permute-done
  362.3 5.4 collective-permute-done
  404.1 5.4 collective-permute-done
  418.0 5.4 collective-permute-done
  432.0 5.4 collective-permute-done
  445.9 5.4 collective-permute-done
  459.8 5.4 collective-permute-done
  473.7 5.4 collective-permute-done
  487.6 5.4 collective-permute-done
  529.4 5.4 collective-permute-done
  543.3 5.4 collective-permute-done
  557.3 5.4 collective-permute-done
  571.2 5.4 collective-permute-done
  585.1 5.4 collective-permute-done
  599.0 5.4 collective-permute-done
  613.0 5.4 collective-permute-done
  626.9 5.4 collective-permute-done
  668.6 5.4 collective-permute-done
  682.6 5.4 collective-permute-done
  696.5 5.4 collective-permute-done
  710.4 5.4 collective-permute-done
  724.3 5.4 collective-permute-done
  738.3 5.4 collective-permute-done
  752.2 5.4 collective-permute-done
  794.0 5.4 collective-permute-done
  807.9 5.4 collective-permute-done
  821.8 5.4 collective-permute-done
  835.7 5.4 collective-permute-done
  849.6 5.4 collective-permute-done
  863.6 5.4 collective-permute-done
  877.5 5.4 collective-permute-done
  891.4 5.4 collective-permute-done
  933.2 5.4 collective-permute-done
  947.1 5.4 collective-permute-done
  1056.0 19.2 %while.29 = (s32[]{:T(128)}, f32[2,512,2,128]{1,0,3,2:T(2,128)S(1)}, s32[2]{0:T(128)S(1)}, f32[1024]{0:T(1024)S(1)}, bf16[1024,2,128]{2,1,0:T(2,128)(2,1)S(1)}, ...) while((s32[]{:T(128)}, ...), condition=%wide.region_1.2_spmd.clone, body=%wide.region_0.1_spmd.clone.sunk | while | flops 540541440 | bytes 5519551 | solution.py:62
  (319 shorter events, 481.9 us)
Async XLA Ops:
  6.5 89.9 %all-gather.3.cloned.1.call-start = ((), (), s32[]{:S(2)}) async-start(), calls=%async_computation | async-start | bytes 3194880 | tf_op jit(solution)/shard_map/all_gather | solution.py:74
  7.3 156.8 %all-gather.5.cloned.1.call-start = ((), (), s32[]{:S(2)}) async-start(), calls=%async_computation.1 | async-start | bytes 4718592 | tf_op jit(solution)/shard_map/all_gather | solution.py:70
  176.5 13.3 %collective-permute-start.1 = (bf16[2,128,128]{2,1,0:T(8,128)(2,1)S(1)}, bf16[2,128,128]{2,1,0:T(8,128)(2,1)S(1)}, u32[]{:S(2)}, u32[]{:S(2)}) collective-permute-start(bf16[2,128,128]{2,1,0:T(8,128)(2,1)S(1)} %get-tuple-element.318), channel_id=1, source_target_pairs={{0,8},{8,16},{16,24},{24,32},{32,40},{40,48},{48,56},{56,64},{64,7... | collective-permute-start | bytes 196616 | tf_op jit(solution)/shard_map/while/body/eval_jaxpr/ppermute | solution.py:12
  190.5 13.3 %collective-permute-start.1 = (bf16[2,128,128]{2,1,0:T(8,128)(2,1)S(1)}, bf16[2,128,128]{2,1,0:T(8,128)(2,1)S(1)}, u32[]{:S(2)}, u32[]{:S(2)}) collective-permute-start(bf16[2,128,128]{2,1,0:T(8,128)(2,1)S(1)} %get-tuple-element.318), channel_id=1, source_target_pairs={{0,8},{8,16},{16,24},{24,32},{32,40},{40,48},{48,56},{56,64},{64,7... | collective-permute-start | bytes 196616 | tf_op jit(solution)/shard_map/while/body/eval_jaxpr/ppermute | solution.py:12
  204.4 13.3 %collective-permute-start.1 = (bf16[2,128,128]{2,1,0:T(8,128)(2,1)S(1)}, bf16[2,128,128]{2,1,0:T(8,128)(2,1)S(1)}, u32[]{:S(2)}, u32[]{:S(2)}) collective-permute-start(bf16[2,128,128]{2,1,0:T(8,128)(2,1)S(1)} %get-tuple-element.318), channel_id=1, source_target_pairs={{0,8},{8,16},{16,24},{24,32},{32,40},{40,48},{48,56},{56,64},{64,7... | collective-permute-start | bytes 196616 | tf_op jit(solution)/shard_map/while/body/eval_jaxpr/ppermute | solution.py:12
  218.3 13.3 %collective-permute-start.1 = (bf16[2,128,128]{2,1,0:T(8,128)(2,1)S(1)}, bf16[2,128,128]{2,1,0:T(8,128)(2,1)S(1)}, u32[]{:S(2)}, u32[]{:S(2)}) collective-permute-start(bf16[2,128,128]{2,1,0:T(8,128)(2,1)S(1)} %get-tuple-element.318), channel_id=1, source_target_pairs={{0,8},{8,16},{16,24},{24,32},{32,40},{40,48},{48,56},{56,64},{64,7... | collective-permute-start | bytes 196616 | tf_op jit(solution)/shard_map/while/body/eval_jaxpr/ppermute | solution.py:12
  232.3 13.3 %collective-permute-start.1 = (bf16[2,128,128]{2,1,0:T(8,128)(2,1)S(1)}, bf16[2,128,128]{2,1,0:T(8,128)(2,1)S(1)}, u32[]{:S(2)}, u32[]{:S(2)}) collective-permute-start(bf16[2,128,128]{2,1,0:T(8,128)(2,1)S(1)} %get-tuple-element.318), channel_id=1, source_target_pairs={{0,8},{8,16},{16,24},{24,32},{32,40},{40,48},{48,56},{56,64},{64,7... | collective-permute-start | bytes 196616 | tf_op jit(solution)/shard_map/while/body/eval_jaxpr/ppermute | solution.py:12
  246.2 13.3 %collective-permute-start.1 = (bf16[2,128,128]{2,1,0:T(8,128)(2,1)S(1)}, bf16[2,128,128]{2,1,0:T(8,128)(2,1)S(1)}, u32[]{:S(2)}, u32[]{:S(2)}) collective-permute-start(bf16[2,128,128]{2,1,0:T(8,128)(2,1)S(1)} %get-tuple-element.318), channel_id=1, source_target_pairs={{0,8},{8,16},{16,24},{24,32},{32,40},{40,48},{48,56},{56,64},{64,7... | collective-permute-start | bytes 196616 | tf_op jit(solution)/shard_map/while/body/eval_jaxpr/ppermute | solution.py:12
  260.1 13.3 %collective-permute-start.1 = (bf16[2,128,128]{2,1,0:T(8,128)(2,1)S(1)}, bf16[2,128,128]{2,1,0:T(8,128)(2,1)S(1)}, u32[]{:S(2)}, u32[]{:S(2)}) collective-permute-start(bf16[2,128,128]{2,1,0:T(8,128)(2,1)S(1)} %get-tuple-element.318), channel_id=1, source_target_pairs={{0,8},{8,16},{16,24},{24,32},{32,40},{40,48},{48,56},{56,64},{64,7... | collective-permute-start | bytes 196616 | tf_op jit(solution)/shard_map/while/body/eval_jaxpr/ppermute | solution.py:12
  274.0 13.3 %collective-permute-start.1 = (bf16[2,128,128]{2,1,0:T(8,128)(2,1)S(1)}, bf16[2,128,128]{2,1,0:T(8,128)(2,1)S(1)}, u32[]{:S(2)}, u32[]{:S(2)}) collective-permute-start(bf16[2,128,128]{2,1,0:T(8,128)(2,1)S(1)} %get-tuple-element.318), channel_id=1, source_target_pairs={{0,8},{8,16},{16,24},{24,32},{32,40},{40,48},{48,56},{56,64},{64,7... | collective-permute-start | bytes 196616 | tf_op jit(solution)/shard_map/while/body/eval_jaxpr/ppermute | solution.py:12
  287.9 13.3 %collective-permute-start.1 = (bf16[2,128,128]{2,1,0:T(8,128)(2,1)S(1)}, bf16[2,128,128]{2,1,0:T(8,128)(2,1)S(1)}, u32[]{:S(2)}, u32[]{:S(2)}) collective-permute-start(bf16[2,128,128]{2,1,0:T(8,128)(2,1)S(1)} %get-tuple-element.318), channel_id=1, source_target_pairs={{0,8},{8,16},{16,24},{24,32},{32,40},{40,48},{48,56},{56,64},{64,7... | collective-permute-start | bytes 196616 | tf_op jit(solution)/shard_map/while/body/eval_jaxpr/ppermute | solution.py:12
  301.9 13.3 %collective-permute-start.1 = (bf16[2,128,128]{2,1,0:T(8,128)(2,1)S(1)}, bf16[2,128,128]{2,1,0:T(8,128)(2,1)S(1)}, u32[]{:S(2)}, u32[]{:S(2)}) collective-permute-start(bf16[2,128,128]{2,1,0:T(8,128)(2,1)S(1)} %get-tuple-element.318), channel_id=1, source_target_pairs={{0,8},{8,16},{16,24},{24,32},{32,40},{40,48},{48,56},{56,64},{64,7... | collective-permute-start | bytes 196616 | tf_op jit(solution)/shard_map/while/body/eval_jaxpr/ppermute | solution.py:12
  315.8 13.3 %collective-permute-start.1 = (bf16[2,128,128]{2,1,0:T(8,128)(2,1)S(1)}, bf16[2,128,128]{2,1,0:T(8,128)(2,1)S(1)}, u32[]{:S(2)}, u32[]{:S(2)}) collective-permute-start(bf16[2,128,128]{2,1,0:T(8,128)(2,1)S(1)} %get-tuple-element.318), channel_id=1, source_target_pairs={{0,8},{8,16},{16,24},{24,32},{32,40},{40,48},{48,56},{56,64},{64,7... | collective-permute-start | bytes 196616 | tf_op jit(solution)/shard_map/while/body/eval_jaxpr/ppermute | solution.py:12
  329.7 13.3 %collective-permute-start.1 = (bf16[2,128,128]{2,1,0:T(8,128)(2,1)S(1)}, bf16[2,128,128]{2,1,0:T(8,128)(2,1)S(1)}, u32[]{:S(2)}, u32[]{:S(2)}) collective-permute-start(bf16[2,128,128]{2,1,0:T(8,128)(2,1)S(1)} %get-tuple-element.318), channel_id=1, source_target_pairs={{0,8},{8,16},{16,24},{24,32},{32,40},{40,48},{48,56},{56,64},{64,7... | collective-permute-start | bytes 196616 | tf_op jit(solution)/shard_map/while/body/eval_jaxpr/ppermute | solution.py:12
  343.6 13.3 %collective-permute-start.1 = (bf16[2,128,128]{2,1,0:T(8,128)(2,1)S(1)}, bf16[2,128,128]{2,1,0:T(8,128)(2,1)S(1)}, u32[]{:S(2)}, u32[]{:S(2)}) collective-permute-start(bf16[2,128,128]{2,1,0:T(8,128)(2,1)S(1)} %get-tuple-element.318), channel_id=1, source_target_pairs={{0,8},{8,16},{16,24},{24,32},{32,40},{40,48},{48,56},{56,64},{64,7... | collective-permute-start | bytes 196616 | tf_op jit(solution)/shard_map/while/body/eval_jaxpr/ppermute | solution.py:12
  357.6 13.3 %collective-permute-start.1 = (bf16[2,128,128]{2,1,0:T(8,128)(2,1)S(1)}, bf16[2,128,128]{2,1,0:T(8,128)(2,1)S(1)}, u32[]{:S(2)}, u32[]{:S(2)}) collective-permute-start(bf16[2,128,128]{2,1,0:T(8,128)(2,1)S(1)} %get-tuple-element.318), channel_id=1, source_target_pairs={{0,8},{8,16},{16,24},{24,32},{32,40},{40,48},{48,56},{56,64},{64,7... | collective-permute-start | bytes 196616 | tf_op jit(solution)/shard_map/while/body/eval_jaxpr/ppermute | solution.py:12
  371.5 13.3 %collective-permute-start.1 = (bf16[2,128,128]{2,1,0:T(8,128)(2,1)S(1)}, bf16[2,128,128]{2,1,0:T(8,128)(2,1)S(1)}, u32[]{:S(2)}, u32[]{:S(2)}) collective-permute-start(bf16[2,128,128]{2,1,0:T(8,128)(2,1)S(1)} %get-tuple-element.318), channel_id=1, source_target_pairs={{0,8},{8,16},{16,24},{24,32},{32,40},{40,48},{48,56},{56,64},{64,7... | collective-permute-start | bytes 196616 | tf_op jit(solution)/shard_map/while/body/eval_jaxpr/ppermute | solution.py:12
  385.4 13.3 %collective-permute-start.1 = (bf16[2,128,128]{2,1,0:T(8,128)(2,1)S(1)}, bf16[2,128,128]{2,1,0:T(8,128)(2,1)S(1)}, u32[]{:S(2)}, u32[]{:S(2)}) collective-permute-start(bf16[2,128,128]{2,1,0:T(8,128)(2,1)S(1)} %get-tuple-element.318), channel_id=1, source_target_pairs={{0,8},{8,16},{16,24},{24,32},{32,40},{40,48},{48,56},{56,64},{64,7... | collective-permute-start | bytes 196616 | tf_op jit(solution)/shard_map/while/body/eval_jaxpr/ppermute | solution.py:12
  399.3 13.3 %collective-permute-start.1 = (bf16[2,128,128]{2,1,0:T(8,128)(2,1)S(1)}, bf16[2,128,128]{2,1,0:T(8,128)(2,1)S(1)}, u32[]{:S(2)}, u32[]{:S(2)}) collective-permute-start(bf16[2,128,128]{2,1,0:T(8,128)(2,1)S(1)} %get-tuple-element.318), channel_id=1, source_target_pairs={{0,8},{8,16},{16,24},{24,32},{32,40},{40,48},{48,56},{56,64},{64,7... | collective-permute-start | bytes 196616 | tf_op jit(solution)/shard_map/while/body/eval_jaxpr/ppermute | solution.py:12
  413.3 13.3 %collective-permute-start.1 = (bf16[2,128,128]{2,1,0:T(8,128)(2,1)S(1)}, bf16[2,128,128]{2,1,0:T(8,128)(2,1)S(1)}, u32[]{:S(2)}, u32[]{:S(2)}) collective-permute-start(bf16[2,128,128]{2,1,0:T(8,128)(2,1)S(1)} %get-tuple-element.318), channel_id=1, source_target_pairs={{0,8},{8,16},{16,24},{24,32},{32,40},{40,48},{48,56},{56,64},{64,7... | collective-permute-start | bytes 196616 | tf_op jit(solution)/shard_map/while/body/eval_jaxpr/ppermute | solution.py:12
  427.2 13.3 %collective-permute-start.1 = (bf16[2,128,128]{2,1,0:T(8,128)(2,1)S(1)}, bf16[2,128,128]{2,1,0:T(8,128)(2,1)S(1)}, u32[]{:S(2)}, u32[]{:S(2)}) collective-permute-start(bf16[2,128,128]{2,1,0:T(8,128)(2,1)S(1)} %get-tuple-element.318), channel_id=1, source_target_pairs={{0,8},{8,16},{16,24},{24,32},{32,40},{40,48},{48,56},{56,64},{64,7... | collective-permute-start | bytes 196616 | tf_op jit(solution)/shard_map/while/body/eval_jaxpr/ppermute | solution.py:12
  441.1 13.3 %collective-permute-start.1 = (bf16[2,128,128]{2,1,0:T(8,128)(2,1)S(1)}, bf16[2,128,128]{2,1,0:T(8,128)(2,1)S(1)}, u32[]{:S(2)}, u32[]{:S(2)}) collective-permute-start(bf16[2,128,128]{2,1,0:T(8,128)(2,1)S(1)} %get-tuple-element.318), channel_id=1, source_target_pairs={{0,8},{8,16},{16,24},{24,32},{32,40},{40,48},{48,56},{56,64},{64,7... | collective-permute-start | bytes 196616 | tf_op jit(solution)/shard_map/while/body/eval_jaxpr/ppermute | solution.py:12
  455.0 13.3 %collective-permute-start.1 = (bf16[2,128,128]{2,1,0:T(8,128)(2,1)S(1)}, bf16[2,128,128]{2,1,0:T(8,128)(2,1)S(1)}, u32[]{:S(2)}, u32[]{:S(2)}) collective-permute-start(bf16[2,128,128]{2,1,0:T(8,128)(2,1)S(1)} %get-tuple-element.318), channel_id=1, source_target_pairs={{0,8},{8,16},{16,24},{24,32},{32,40},{40,48},{48,56},{56,64},{64,7... | collective-permute-start | bytes 196616 | tf_op jit(solution)/shard_map/while/body/eval_jaxpr/ppermute | solution.py:12
  468.9 13.3 %collective-permute-start.1 = (bf16[2,128,128]{2,1,0:T(8,128)(2,1)S(1)}, bf16[2,128,128]{2,1,0:T(8,128)(2,1)S(1)}, u32[]{:S(2)}, u32[]{:S(2)}) collective-permute-start(bf16[2,128,128]{2,1,0:T(8,128)(2,1)S(1)} %get-tuple-element.318), channel_id=1, source_target_pairs={{0,8},{8,16},{16,24},{24,32},{32,40},{40,48},{48,56},{56,64},{64,7... | collective-permute-start | bytes 196616 | tf_op jit(solution)/shard_map/while/body/eval_jaxpr/ppermute | solution.py:12
  482.9 13.3 %collective-permute-start.1 = (bf16[2,128,128]{2,1,0:T(8,128)(2,1)S(1)}, bf16[2,128,128]{2,1,0:T(8,128)(2,1)S(1)}, u32[]{:S(2)}, u32[]{:S(2)}) collective-permute-start(bf16[2,128,128]{2,1,0:T(8,128)(2,1)S(1)} %get-tuple-element.318), channel_id=1, source_target_pairs={{0,8},{8,16},{16,24},{24,32},{32,40},{40,48},{48,56},{56,64},{64,7... | collective-permute-start | bytes 196616 | tf_op jit(solution)/shard_map/while/body/eval_jaxpr/ppermute | solution.py:12
  496.8 13.3 %collective-permute-start.1 = (bf16[2,128,128]{2,1,0:T(8,128)(2,1)S(1)}, bf16[2,128,128]{2,1,0:T(8,128)(2,1)S(1)}, u32[]{:S(2)}, u32[]{:S(2)}) collective-permute-start(bf16[2,128,128]{2,1,0:T(8,128)(2,1)S(1)} %get-tuple-element.318), channel_id=1, source_target_pairs={{0,8},{8,16},{16,24},{24,32},{32,40},{40,48},{48,56},{56,64},{64,7... | collective-permute-start | bytes 196616 | tf_op jit(solution)/shard_map/while/body/eval_jaxpr/ppermute | solution.py:12
  552.5 13.3 %collective-permute-start.1 = (bf16[2,128,128]{2,1,0:T(8,128)(2,1)S(1)}, bf16[2,128,128]{2,1,0:T(8,128)(2,1)S(1)}, u32[]{:S(2)}, u32[]{:S(2)}) collective-permute-start(bf16[2,128,128]{2,1,0:T(8,128)(2,1)S(1)} %get-tuple-element.318), channel_id=1, source_target_pairs={{0,8},{8,16},{16,24},{24,32},{32,40},{40,48},{48,56},{56,64},{64,7... | collective-permute-start | bytes 196616 | tf_op jit(solution)/shard_map/while/body/eval_jaxpr/ppermute | solution.py:12
  566.4 13.3 %collective-permute-start.1 = (bf16[2,128,128]{2,1,0:T(8,128)(2,1)S(1)}, bf16[2,128,128]{2,1,0:T(8,128)(2,1)S(1)}, u32[]{:S(2)}, u32[]{:S(2)}) collective-permute-start(bf16[2,128,128]{2,1,0:T(8,128)(2,1)S(1)} %get-tuple-element.318), channel_id=1, source_target_pairs={{0,8},{8,16},{16,24},{24,32},{32,40},{40,48},{48,56},{56,64},{64,7... | collective-permute-start | bytes 196616 | tf_op jit(solution)/shard_map/while/body/eval_jaxpr/ppermute | solution.py:12
  580.3 13.3 %collective-permute-start.1 = (bf16[2,128,128]{2,1,0:T(8,128)(2,1)S(1)}, bf16[2,128,128]{2,1,0:T(8,128)(2,1)S(1)}, u32[]{:S(2)}, u32[]{:S(2)}) collective-permute-start(bf16[2,128,128]{2,1,0:T(8,128)(2,1)S(1)} %get-tuple-element.318), channel_id=1, source_target_pairs={{0,8},{8,16},{16,24},{24,32},{32,40},{40,48},{48,56},{56,64},{64,7... | collective-permute-start | bytes 196616 | tf_op jit(solution)/shard_map/while/body/eval_jaxpr/ppermute | solution.py:12
  594.3 13.3 %collective-permute-start.1 = (bf16[2,128,128]{2,1,0:T(8,128)(2,1)S(1)}, bf16[2,128,128]{2,1,0:T(8,128)(2,1)S(1)}, u32[]{:S(2)}, u32[]{:S(2)}) collective-permute-start(bf16[2,128,128]{2,1,0:T(8,128)(2,1)S(1)} %get-tuple-element.318), channel_id=1, source_target_pairs={{0,8},{8,16},{16,24},{24,32},{32,40},{40,48},{48,56},{56,64},{64,7... | collective-permute-start | bytes 196616 | tf_op jit(solution)/shard_map/while/body/eval_jaxpr/ppermute | solution.py:12
  608.2 13.3 %collective-permute-start.1 = (bf16[2,128,128]{2,1,0:T(8,128)(2,1)S(1)}, bf16[2,128,128]{2,1,0:T(8,128)(2,1)S(1)}, u32[]{:S(2)}, u32[]{:S(2)}) collective-permute-start(bf16[2,128,128]{2,1,0:T(8,128)(2,1)S(1)} %get-tuple-element.318), channel_id=1, source_target_pairs={{0,8},{8,16},{16,24},{24,32},{32,40},{40,48},{48,56},{56,64},{64,7... | collective-permute-start | bytes 196616 | tf_op jit(solution)/shard_map/while/body/eval_jaxpr/ppermute | solution.py:12
  677.8 13.3 %collective-permute-start.1 = (bf16[2,128,128]{2,1,0:T(8,128)(2,1)S(1)}, bf16[2,128,128]{2,1,0:T(8,128)(2,1)S(1)}, u32[]{:S(2)}, u32[]{:S(2)}) collective-permute-start(bf16[2,128,128]{2,1,0:T(8,128)(2,1)S(1)} %get-tuple-element.318), channel_id=1, source_target_pairs={{0,8},{8,16},{16,24},{24,32},{32,40},{40,48},{48,56},{56,64},{64,7... | collective-permute-start | bytes 196616 | tf_op jit(solution)/shard_map/while/body/eval_jaxpr/ppermute | solution.py:12
  691.7 13.3 %collective-permute-start.1 = (bf16[2,128,128]{2,1,0:T(8,128)(2,1)S(1)}, bf16[2,128,128]{2,1,0:T(8,128)(2,1)S(1)}, u32[]{:S(2)}, u32[]{:S(2)}) collective-permute-start(bf16[2,128,128]{2,1,0:T(8,128)(2,1)S(1)} %get-tuple-element.318), channel_id=1, source_target_pairs={{0,8},{8,16},{16,24},{24,32},{32,40},{40,48},{48,56},{56,64},{64,7... | collective-permute-start | bytes 196616 | tf_op jit(solution)/shard_map/while/body/eval_jaxpr/ppermute | solution.py:12
  705.6 13.3 %collective-permute-start.1 = (bf16[2,128,128]{2,1,0:T(8,128)(2,1)S(1)}, bf16[2,128,128]{2,1,0:T(8,128)(2,1)S(1)}, u32[]{:S(2)}, u32[]{:S(2)}) collective-permute-start(bf16[2,128,128]{2,1,0:T(8,128)(2,1)S(1)} %get-tuple-element.318), channel_id=1, source_target_pairs={{0,8},{8,16},{16,24},{24,32},{32,40},{40,48},{48,56},{56,64},{64,7... | collective-permute-start | bytes 196616 | tf_op jit(solution)/shard_map/while/body/eval_jaxpr/ppermute | solution.py:12
  719.6 13.3 %collective-permute-start.1 = (bf16[2,128,128]{2,1,0:T(8,128)(2,1)S(1)}, bf16[2,128,128]{2,1,0:T(8,128)(2,1)S(1)}, u32[]{:S(2)}, u32[]{:S(2)}) collective-permute-start(bf16[2,128,128]{2,1,0:T(8,128)(2,1)S(1)} %get-tuple-element.318), channel_id=1, source_target_pairs={{0,8},{8,16},{16,24},{24,32},{32,40},{40,48},{48,56},{56,64},{64,7... | collective-permute-start | bytes 196616 | tf_op jit(solution)/shard_map/while/body/eval_jaxpr/ppermute | solution.py:12
  733.5 13.3 %collective-permute-start.1 = (bf16[2,128,128]{2,1,0:T(8,128)(2,1)S(1)}, bf16[2,128,128]{2,1,0:T(8,128)(2,1)S(1)}, u32[]{:S(2)}, u32[]{:S(2)}) collective-permute-start(bf16[2,128,128]{2,1,0:T(8,128)(2,1)S(1)} %get-tuple-element.318), channel_id=1, source_target_pairs={{0,8},{8,16},{16,24},{24,32},{32,40},{40,48},{48,56},{56,64},{64,7... | collective-permute-start | bytes 196616 | tf_op jit(solution)/shard_map/while/body/eval_jaxpr/ppermute | solution.py:12
  747.4 13.3 %collective-permute-start.1 = (bf16[2,128,128]{2,1,0:T(8,128)(2,1)S(1)}, bf16[2,128,128]{2,1,0:T(8,128)(2,1)S(1)}, u32[]{:S(2)}, u32[]{:S(2)}) collective-permute-start(bf16[2,128,128]{2,1,0:T(8,128)(2,1)S(1)} %get-tuple-element.318), channel_id=1, source_target_pairs={{0,8},{8,16},{16,24},{24,32},{32,40},{40,48},{48,56},{56,64},{64,7... | collective-permute-start | bytes 196616 | tf_op jit(solution)/shard_map/while/body/eval_jaxpr/ppermute | solution.py:12
  817.0 13.3 %collective-permute-start.1 = (bf16[2,128,128]{2,1,0:T(8,128)(2,1)S(1)}, bf16[2,128,128]{2,1,0:T(8,128)(2,1)S(1)}, u32[]{:S(2)}, u32[]{:S(2)}) collective-permute-start(bf16[2,128,128]{2,1,0:T(8,128)(2,1)S(1)} %get-tuple-element.318), channel_id=1, source_target_pairs={{0,8},{8,16},{16,24},{24,32},{32,40},{40,48},{48,56},{56,64},{64,7... | collective-permute-start | bytes 196616 | tf_op jit(solution)/shard_map/while/body/eval_jaxpr/ppermute | solution.py:12
  830.9 13.3 %collective-permute-start.1 = (bf16[2,128,128]{2,1,0:T(8,128)(2,1)S(1)}, bf16[2,128,128]{2,1,0:T(8,128)(2,1)S(1)}, u32[]{:S(2)}, u32[]{:S(2)}) collective-permute-start(bf16[2,128,128]{2,1,0:T(8,128)(2,1)S(1)} %get-tuple-element.318), channel_id=1, source_target_pairs={{0,8},{8,16},{16,24},{24,32},{32,40},{40,48},{48,56},{56,64},{64,7... | collective-permute-start | bytes 196616 | tf_op jit(solution)/shard_map/while/body/eval_jaxpr/ppermute | solution.py:12
  844.9 13.3 %collective-permute-start.1 = (bf16[2,128,128]{2,1,0:T(8,128)(2,1)S(1)}, bf16[2,128,128]{2,1,0:T(8,128)(2,1)S(1)}, u32[]{:S(2)}, u32[]{:S(2)}) collective-permute-start(bf16[2,128,128]{2,1,0:T(8,128)(2,1)S(1)} %get-tuple-element.318), channel_id=1, source_target_pairs={{0,8},{8,16},{16,24},{24,32},{32,40},{40,48},{48,56},{56,64},{64,7... | collective-permute-start | bytes 196616 | tf_op jit(solution)/shard_map/while/body/eval_jaxpr/ppermute | solution.py:12
  858.8 13.3 %collective-permute-start.1 = (bf16[2,128,128]{2,1,0:T(8,128)(2,1)S(1)}, bf16[2,128,128]{2,1,0:T(8,128)(2,1)S(1)}, u32[]{:S(2)}, u32[]{:S(2)}) collective-permute-start(bf16[2,128,128]{2,1,0:T(8,128)(2,1)S(1)} %get-tuple-element.318), channel_id=1, source_target_pairs={{0,8},{8,16},{16,24},{24,32},{32,40},{40,48},{48,56},{56,64},{64,7... | collective-permute-start | bytes 196616 | tf_op jit(solution)/shard_map/while/body/eval_jaxpr/ppermute | solution.py:12
  872.7 13.3 %collective-permute-start.1 = (bf16[2,128,128]{2,1,0:T(8,128)(2,1)S(1)}, bf16[2,128,128]{2,1,0:T(8,128)(2,1)S(1)}, u32[]{:S(2)}, u32[]{:S(2)}) collective-permute-start(bf16[2,128,128]{2,1,0:T(8,128)(2,1)S(1)} %get-tuple-element.318), channel_id=1, source_target_pairs={{0,8},{8,16},{16,24},{24,32},{32,40},{40,48},{48,56},{56,64},{64,7... | collective-permute-start | bytes 196616 | tf_op jit(solution)/shard_map/while/body/eval_jaxpr/ppermute | solution.py:12
  942.3 13.3 %collective-permute-start.1 = (bf16[2,128,128]{2,1,0:T(8,128)(2,1)S(1)}, bf16[2,128,128]{2,1,0:T(8,128)(2,1)S(1)}, u32[]{:S(2)}, u32[]{:S(2)}) collective-permute-start(bf16[2,128,128]{2,1,0:T(8,128)(2,1)S(1)} %get-tuple-element.318), channel_id=1, source_target_pairs={{0,8},{8,16},{16,24},{24,32},{32,40},{40,48},{48,56},{56,64},{64,7... | collective-permute-start | bytes 196616 | tf_op jit(solution)/shard_map/while/body/eval_jaxpr/ppermute | solution.py:12
  956.3 13.3 %collective-permute-start.1 = (bf16[2,128,128]{2,1,0:T(8,128)(2,1)S(1)}, bf16[2,128,128]{2,1,0:T(8,128)(2,1)S(1)}, u32[]{:S(2)}, u32[]{:S(2)}) collective-permute-start(bf16[2,128,128]{2,1,0:T(8,128)(2,1)S(1)} %get-tuple-element.318), channel_id=1, source_target_pairs={{0,8},{8,16},{16,24},{24,32},{32,40},{40,48},{48,56},{56,64},{64,7... | collective-permute-start | bytes 196616 | tf_op jit(solution)/shard_map/while/body/eval_jaxpr/ppermute | solution.py:12
  970.2 13.3 %collective-permute-start.1 = (bf16[2,128,128]{2,1,0:T(8,128)(2,1)S(1)}, bf16[2,128,128]{2,1,0:T(8,128)(2,1)S(1)}, u32[]{:S(2)}, u32[]{:S(2)}) collective-permute-start(bf16[2,128,128]{2,1,0:T(8,128)(2,1)S(1)} %get-tuple-element.318), channel_id=1, source_target_pairs={{0,8},{8,16},{16,24},{24,32},{32,40},{40,48},{48,56},{56,64},{64,7... | collective-permute-start | bytes 196616 | tf_op jit(solution)/shard_map/while/body/eval_jaxpr/ppermute | solution.py:12
  984.1 13.3 %collective-permute-start.1 = (bf16[2,128,128]{2,1,0:T(8,128)(2,1)S(1)}, bf16[2,128,128]{2,1,0:T(8,128)(2,1)S(1)}, u32[]{:S(2)}, u32[]{:S(2)}) collective-permute-start(bf16[2,128,128]{2,1,0:T(8,128)(2,1)S(1)} %get-tuple-element.318), channel_id=1, source_target_pairs={{0,8},{8,16},{16,24},{24,32},{32,40},{40,48},{48,56},{56,64},{64,7... | collective-permute-start | bytes 196616 | tf_op jit(solution)/shard_map/while/body/eval_jaxpr/ppermute | solution.py:12
  998.0 13.3 %collective-permute-start.1 = (bf16[2,128,128]{2,1,0:T(8,128)(2,1)S(1)}, bf16[2,128,128]{2,1,0:T(8,128)(2,1)S(1)}, u32[]{:S(2)}, u32[]{:S(2)}) collective-permute-start(bf16[2,128,128]{2,1,0:T(8,128)(2,1)S(1)} %get-tuple-element.318), channel_id=1, source_target_pairs={{0,8},{8,16},{16,24},{24,32},{32,40},{40,48},{48,56},{56,64},{64,7... | collective-permute-start | bytes 196616 | tf_op jit(solution)/shard_map/while/body/eval_jaxpr/ppermute | solution.py:12
  1011.9 13.3 %collective-permute-start.1 = (bf16[2,128,128]{2,1,0:T(8,128)(2,1)S(1)}, bf16[2,128,128]{2,1,0:T(8,128)(2,1)S(1)}, u32[]{:S(2)}, u32[]{:S(2)}) collective-permute-start(bf16[2,128,128]{2,1,0:T(8,128)(2,1)S(1)} %get-tuple-element.318), channel_id=1, source_target_pairs={{0,8},{8,16},{16,24},{24,32},{32,40},{40,48},{48,56},{56,64},{64,7... | collective-permute-start | bytes 196616 | tf_op jit(solution)/shard_map/while/body/eval_jaxpr/ppermute | solution.py:12
  (84 other events, 2531.3 us)
Sparse Core Ops, SparseCore 0:
  10.8 85.6 all-gather.2
  98.5 65.5 all-gather.4
where the time goes:
time: 1090 us; the launch traced here: 1080 us
  waiting for transfers between devices  494 us (45%)
  starting transfers between devices  302 us (28%)
  loops' own time  196 us (18%)
  other arithmetic  50.1 us (5%)
  local copies, waits for them, and re-layouts  16.1 us (1%)
  between operations  14.9 us (1%)
  matrix products  11.9 us (1%)
    ppermute x126, waiting for transfers between devices, passed_along(): lax.ppermute(value, axis, [(source, source + steps) for source in range(l...  340 us
    ppermute x126, starting transfers between devices, passed_along(): lax.ppermute(value, axis, [(source, source + steps) for source in range(l...  302 us
    another operation x1, loops' own time, per_device(): lax.fori_loop(0, lax.axis_size('ctx') - 1, hand_round, (own_pair, start_p...  194 us
    all_gather x1, waiting for transfers between devices, per_device(): lax.all_gather(w_qkv, 'ctx', axis=1, tiled=True)  84.4 us
    all_gather x1, waiting for transfers between devices, per_device(): whole = lax.all_gather(tokens, 'head', axis=1, tiled=True)  67.6 us
    add x63, other arithmetic, combine(): later_state + jnp.where(linked, first_state, 0.0)  40.5 us
  transfers between devices with their start and end apart: 128, of which 65 were waited for; matrix products, arithmetic and copies ran while one was open for 0% of the time, Pallas kernels for 0%

commit v1 on v0

--- a/solution.py
+++ b/solution.py
@@ -4,6 +4,14 @@
 from jax.sharding import PartitionSpec as P
 
 HEAD_DIM = 128
+
+
+def gather_by_exchange(array, axis, dim):
+    size = lax.axis_size(axis)
+    repeats = [size if d == dim else 1 for d in range(array.ndim)]
+    return lax.all_to_all(
+        jnp.tile(array, repeats), axis, split_axis=dim, concat_axis=dim, tiled=True
+    )
 
 
 def passed_along(value, axis, steps):
@@ -71,7 +79,7 @@
     projected = jnp.einsum(
         "tr,grc->gtc",
         whole,
-        lax.all_gather(w_qkv, "ctx", axis=1, tiled=True),
+        gather_by_exchange(w_qkv, "ctx", 1),
         preferred_element_type=jnp.float32,
     ).astype(jnp.bfloat16)
     queries, key_map, values, seg_float, kv_state, tail_id = prepare(projected, seg_ids)

time: 1090 us -> 1050 us (0.963)
  waiting for transfers between devices: 494 us -> 430 us
  local copies, waits for them, and re-layouts: 16.1 us -> 34.5 us
  loops' own time: 196 us -> 208 us
    all_to_all x0 -> x1, waiting for transfers between devices: none -> 88.8 us  [gather_by_exchange(): lax.all_to_all(jnp.tile(array, repeats), axis, split_axis=dim, concat_axi...]
    all_gather x1 -> x0, waiting for transfers between devices: 84.4 us -> none  [per_device(): lax.all_gather(w_qkv, 'ctx', axis=1, tiled=True)]
    all_gather x1, waiting for transfers between devices: 67.6 us -> 0.01 us  [per_device(): whole = lax.all_gather(tokens, 'head', axis=1, tiled=True)]
    another operation x0 -> x2, local copies, waits for them, and re-layouts: none -> 18.3 us  [gather_by_exchange(): jnp.tile(array, repeats)]
    another operation x1, loops' own time: 194 us -> 206 us  [per_device(): lax.fori_loop(0, lax.axis_size('ctx') - 1, hand_round, (own_pair, start_p...]
  transfers between devices with their start and end apart: 128 -> 128, of which waited for: 65 -> 64; matrix products, arithmetic and copies ran while one was open for 0% -> 2% of each run, Pallas kernels for 0% -> 0%
where the time goes in v1:
time: 1050 us
  waiting for transfers between devices  430 us (41%)
  starting transfers between devices  303 us (29%)
  loops' own time  208 us (20%)
  other arithmetic  43.2 us (4%)
  local copies, waits for them, and re-layouts  34.5 us (3%)
  between operations  15 us (1%)
  matrix products  12.4 us (1%)
    ppermute x126, waiting for transfers between devices, passed_along(): lax.ppermute(value, axis, [(source, source + steps) for source in range(l...  341 us
    ppermute x126, starting transfers between devices, passed_along(): lax.ppermute(value, axis, [(source, source + steps) for source in range(l...  292 us
    another operation x1, loops' own time, per_device(): lax.fori_loop(0, lax.axis_size('ctx') - 1, hand_round, (own_pair, start_p...  206 us
    all_to_all x1, waiting for transfers between devices, gather_by_exchange(): lax.all_to_all(jnp.tile(array, repeats), axis, split_axis=dim, concat_axi...  88.8 us
    add x63, other arithmetic, combine(): later_state + jnp.where(linked, first_state, 0.0)  40.5 us
  transfers between devices with their start and end apart: 128, of which 64 were waited for; matrix products, arithmetic and copies ran while one was open for 2% of the time, Pallas kernels for 0%

profile of v1, /device:TPU:32, one launch (start us, length us, event | category | flops | bytes accessed | tf_op | source)
XLA Modules:
  0.0 1045.7 jit_solution(8556572639734646609)
XLA Ops:
  8.4 17.2 %copy.33 = bf16[3,2048,256]{2,0,1:T(4,128)(2,1)} copy(bf16[3,2048,256]{2,1,0:T(8,128)(2,1)S(1)} %bitcast.42) | data formatting | bytes 6291456 | tf_op jit(solution)/shard_map/tile | solution.py:13
  25.6 10.9 %all-to-all-start = ((bf16[3,2048,256]{2,0,1:T(4,128)(2,1)}), bf16[3,2048,256]{2,0,1:T(4,128)(2,1)}, u32[]{:S(2)}, u32[]{:S(2)}) async-start(bf16[3,2048,256]{2,0,1:T(4,128)(2,1)} %copy.33), calls=%async_computation | async-start | bytes 8388608 | tf_op jit(solution)/shard_map/all_to_all | solution.py:12
  39.3 88.8 %all-to-all-done = bf16[3,2048,256]{2,0,1:T(4,128)(2,1)} async-done(((bf16[3,2048,256]{2,0,1:T(4,128)(2,1)}), bf16[3,2048,256]{2,0,1:T(4,128)(2,1)}, u32[]{:S(2)}, u32[]{:S(2)}) %all-to-all-start) | async-done | bytes 3145760 | tf_op jit(solution)/shard_map/all_to_all | solution.py:12
  128.0 6.9 fusion.18
  138.2 879.7 %while.28 = (s32[]{:T(128)}, bf16[2,128,128]{2,1,0:T(8,128)(2,1)S(1)}, bf16[]{:T(256)}, bf16[2,128,128]{2,1,0:T(8,128)(2,1)}, f32[]{:T(128)}, /*index=5*/f32[]{:...) while((s32[]{:T(128)}, bf16[2,128,128]{2,1,0:T(8,128)(2,1)S(1)}, bf16[]{:T(256)}, ...), condition=%wide.region_3.4_spmd, body=%wide.region_2.3_spmd.sunk | while | flops 163846 | bytes 590031 | solution.py:98
  156.9 5.4 collective-permute-done
  170.8 5.4 collective-permute-done
  184.8 5.4 collective-permute-done
  198.8 5.4 collective-permute-done
  212.7 5.4 collective-permute-done
  226.7 5.4 collective-permute-done
  240.7 5.4 collective-permute-done
  254.6 5.4 collective-permute-done
  268.6 5.4 collective-permute-done
  282.5 5.4 collective-permute-done
  296.5 5.4 collective-permute-done
  310.5 5.4 collective-permute-done
  324.4 5.4 collective-permute-done
  338.4 5.4 collective-permute-done
  352.3 5.4 collective-permute-done
  366.3 5.4 collective-permute-done
  380.3 5.4 collective-permute-done
  394.2 5.4 collective-permute-done
  408.2 5.4 collective-permute-done
  422.2 5.4 collective-permute-done
  436.1 5.4 collective-permute-done
  450.1 5.4 collective-permute-done
  464.0 5.4 collective-permute-done
  478.0 5.4 collective-permute-done
  492.0 5.4 collective-permute-done
  505.9 5.4 collective-permute-done
  519.9 5.4 collective-permute-done
  533.8 5.4 collective-permute-done
  547.8 5.4 collective-permute-done
  561.8 5.4 collective-permute-done
  575.7 5.4 collective-permute-done
  589.7 5.4 collective-permute-done
  603.7 5.4 collective-permute-done
  617.6 5.4 collective-permute-done
  631.6 5.4 collective-permute-done
  645.5 5.4 collective-permute-done
  659.5 5.4 collective-permute-done
  673.5 5.4 collective-permute-done
  687.4 5.4 collective-permute-done
  841.0 5.4 collective-permute-done
  855.0 5.4 collective-permute-done
  868.9 5.4 collective-permute-done
  1017.9 18.5 %while.29 = (s32[]{:T(128)}, f32[2,512,2,128]{1,0,3,2:T(2,128)S(1)}, s32[2]{0:T(128)S(1)}, f32[1024]{0:T(1024)S(1)}, bf16[1024,2,128]{2,0,1:T(8,128)(2,1)S(1)}, ...) while((s32[]{:T(128)}, ...), condition=%wide.region_1.2_spmd.clone, body=%wide.region_0.1_spmd.clone.sunk | while | flops 540541440 | bytes 4995255 | solution.py:70
  (321 shorter events, 472.4 us)
Async XLA Ops:
  6.5 121.5 %all-gather.2.cloned.1.call-start = ((), (), s32[]{:S(2)}) async-start(), calls=%async_computation.1 | async-start | bytes 4718592 | tf_op jit(solution)/shard_map/all_gather | solution.py:78
  25.6 102.4 %all-to-all-start = ((bf16[3,2048,256]{2,0,1:T(4,128)(2,1)}), bf16[3,2048,256]{2,0,1:T(4,128)(2,1)}, u32[]{:S(2)}, u32[]{:S(2)}) async-start(bf16[3,2048,256]{2,0,1:T(4,128)(2,1)} %copy.33), calls=%async_computation | async-start | bytes 8388608 | tf_op jit(solution)/shard_map/all_to_all | solution.py:12
  138.2 13.4 %collective-permute-start.1 = (bf16[2,128,128]{2,1,0:T(8,128)(2,1)S(1)}, bf16[2,128,128]{2,1,0:T(8,128)(2,1)S(1)}, u32[]{:S(2)}, u32[]{:S(2)}) collective-permute-start(bf16[2,128,128]{2,1,0:T(8,128)(2,1)S(1)} %get-tuple-element.332), channel_id=1, source_target_pairs={{0,8},{8,16},{16,24},{24,32},{32,40},{40,48},{48,56},{56,64},{64,7... | collective-permute-start | bytes 196616 | tf_op jit(solution)/shard_map/while/body/eval_jaxpr/ppermute | solution.py:20
  152.2 13.3 %collective-permute-start.1 = (bf16[2,128,128]{2,1,0:T(8,128)(2,1)S(1)}, bf16[2,128,128]{2,1,0:T(8,128)(2,1)S(1)}, u32[]{:S(2)}, u32[]{:S(2)}) collective-permute-start(bf16[2,128,128]{2,1,0:T(8,128)(2,1)S(1)} %get-tuple-element.332), channel_id=1, source_target_pairs={{0,8},{8,16},{16,24},{24,32},{32,40},{40,48},{48,56},{56,64},{64,7... | collective-permute-start | bytes 196616 | tf_op jit(solution)/shard_map/while/body/eval_jaxpr/ppermute | solution.py:20
  166.2 13.3 %collective-permute-start.1 = (bf16[2,128,128]{2,1,0:T(8,128)(2,1)S(1)}, bf16[2,128,128]{2,1,0:T(8,128)(2,1)S(1)}, u32[]{:S(2)}, u32[]{:S(2)}) collective-permute-start(bf16[2,128,128]{2,1,0:T(8,128)(2,1)S(1)} %get-tuple-element.332), channel_id=1, source_target_pairs={{0,8},{8,16},{16,24},{24,32},{32,40},{40,48},{48,56},{56,64},{64,7... | collective-permute-start | bytes 196616 | tf_op jit(solution)/shard_map/while/body/eval_jaxpr/ppermute | solution.py:20
  180.2 13.3 %collective-permute-start.1 = (bf16[2,128,128]{2,1,0:T(8,128)(2,1)S(1)}, bf16[2,128,128]{2,1,0:T(8,128)(2,1)S(1)}, u32[]{:S(2)}, u32[]{:S(2)}) collective-permute-start(bf16[2,128,128]{2,1,0:T(8,128)(2,1)S(1)} %get-tuple-element.332), channel_id=1, source_target_pairs={{0,8},{8,16},{16,24},{24,32},{32,40},{40,48},{48,56},{56,64},{64,7... | collective-permute-start | bytes 196616 | tf_op jit(solution)/shard_map/while/body/eval_jaxpr/ppermute | solution.py:20
  194.1 13.3 %collective-permute-start.1 = (bf16[2,128,128]{2,1,0:T(8,128)(2,1)S(1)}, bf16[2,128,128]{2,1,0:T(8,128)(2,1)S(1)}, u32[]{:S(2)}, u32[]{:S(2)}) collective-permute-start(bf16[2,128,128]{2,1,0:T(8,128)(2,1)S(1)} %get-tuple-element.332), channel_id=1, source_target_pairs={{0,8},{8,16},{16,24},{24,32},{32,40},{40,48},{48,56},{56,64},{64,7... | collective-permute-start | bytes 196616 | tf_op jit(solution)/shard_map/while/body/eval_jaxpr/ppermute | solution.py:20
  208.1 13.3 %collective-permute-start.1 = (bf16[2,128,128]{2,1,0:T(8,128)(2,1)S(1)}, bf16[2,128,128]{2,1,0:T(8,128)(2,1)S(1)}, u32[]{:S(2)}, u32[]{:S(2)}) collective-permute-start(bf16[2,128,128]{2,1,0:T(8,128)(2,1)S(1)} %get-tuple-element.332), channel_id=1, source_target_pairs={{0,8},{8,16},{16,24},{24,32},{32,40},{40,48},{48,56},{56,64},{64,7... | collective-permute-start | bytes 196616 | tf_op jit(solution)/shard_map/while/body/eval_jaxpr/ppermute | solution.py:20
  222.0 13.3 %collective-permute-start.1 = (bf16[2,128,128]{2,1,0:T(8,128)(2,1)S(1)}, bf16[2,128,128]{2,1,0:T(8,128)(2,1)S(1)}, u32[]{:S(2)}, u32[]{:S(2)}) collective-permute-start(bf16[2,128,128]{2,1,0:T(8,128)(2,1)S(1)} %get-tuple-element.332), channel_id=1, source_target_pairs={{0,8},{8,16},{16,24},{24,32},{32,40},{40,48},{48,56},{56,64},{64,7... | collective-permute-start | bytes 196616 | tf_op jit(solution)/shard_map/while/body/eval_jaxpr/ppermute | solution.py:20
  236.0 13.3 %collective-permute-start.1 = (bf16[2,128,128]{2,1,0:T(8,128)(2,1)S(1)}, bf16[2,128,128]{2,1,0:T(8,128)(2,1)S(1)}, u32[]{:S(2)}, u32[]{:S(2)}) collective-permute-start(bf16[2,128,128]{2,1,0:T(8,128)(2,1)S(1)} %get-tuple-element.332), channel_id=1, source_target_pairs={{0,8},{8,16},{16,24},{24,32},{32,40},{40,48},{48,56},{56,64},{64,7... | collective-permute-start | bytes 196616 | tf_op jit(solution)/shard_map/while/body/eval_jaxpr/ppermute | solution.py:20
  250.0 13.3 %collective-permute-start.1 = (bf16[2,128,128]{2,1,0:T(8,128)(2,1)S(1)}, bf16[2,128,128]{2,1,0:T(8,128)(2,1)S(1)}, u32[]{:S(2)}, u32[]{:S(2)}) collective-permute-start(bf16[2,128,128]{2,1,0:T(8,128)(2,1)S(1)} %get-tuple-element.332), channel_id=1, source_target_pairs={{0,8},{8,16},{16,24},{24,32},{32,40},{40,48},{48,56},{56,64},{64,7... | collective-permute-start | bytes 196616 | tf_op jit(solution)/shard_map/while/body/eval_jaxpr/ppermute | solution.py:20
  263.9 13.3 %collective-permute-start.1 = (bf16[2,128,128]{2,1,0:T(8,128)(2,1)S(1)}, bf16[2,128,128]{2,1,0:T(8,128)(2,1)S(1)}, u32[]{:S(2)}, u32[]{:S(2)}) collective-permute-start(bf16[2,128,128]{2,1,0:T(8,128)(2,1)S(1)} %get-tuple-element.332), channel_id=1, source_target_pairs={{0,8},{8,16},{16,24},{24,32},{32,40},{40,48},{48,56},{56,64},{64,7... | collective-permute-start | bytes 196616 | tf_op jit(solution)/shard_map/while/body/eval_jaxpr/ppermute | solution.py:20
  277.9 13.3 %collective-permute-start.1 = (bf16[2,128,128]{2,1,0:T(8,128)(2,1)S(1)}, bf16[2,128,128]{2,1,0:T(8,128)(2,1)S(1)}, u32[]{:S(2)}, u32[]{:S(2)}) collective-permute-start(bf16[2,128,128]{2,1,0:T(8,128)(2,1)S(1)} %get-tuple-element.332), channel_id=1, source_target_pairs={{0,8},{8,16},{16,24},{24,32},{32,40},{40,48},{48,56},{56,64},{64,7... | collective-permute-start | bytes 196616 | tf_op jit(solution)/shard_map/while/body/eval_jaxpr/ppermute | solution.py:20
  333.7 13.3 %collective-permute-start.1 = (bf16[2,128,128]{2,1,0:T(8,128)(2,1)S(1)}, bf16[2,128,128]{2,1,0:T(8,128)(2,1)S(1)}, u32[]{:S(2)}, u32[]{:S(2)}) collective-permute-start(bf16[2,128,128]{2,1,0:T(8,128)(2,1)S(1)} %get-tuple-element.332), channel_id=1, source_target_pairs={{0,8},{8,16},{16,24},{24,32},{32,40},{40,48},{48,56},{56,64},{64,7... | collective-permute-start | bytes 196616 | tf_op jit(solution)/shard_map/while/body/eval_jaxpr/ppermute | solution.py:20
  347.7 13.3 %collective-permute-start.1 = (bf16[2,128,128]{2,1,0:T(8,128)(2,1)S(1)}, bf16[2,128,128]{2,1,0:T(8,128)(2,1)S(1)}, u32[]{:S(2)}, u32[]{:S(2)}) collective-permute-start(bf16[2,128,128]{2,1,0:T(8,128)(2,1)S(1)} %get-tuple-element.332), channel_id=1, source_target_pairs={{0,8},{8,16},{16,24},{24,32},{32,40},{40,48},{48,56},{56,64},{64,7... | collective-permute-start | bytes 196616 | tf_op jit(solution)/shard_map/while/body/eval_jaxpr/ppermute | solution.py:20
  361.7 13.3 %collective-permute-start.1 = (bf16[2,128,128]{2,1,0:T(8,128)(2,1)S(1)}, bf16[2,128,128]{2,1,0:T(8,128)(2,1)S(1)}, u32[]{:S(2)}, u32[]{:S(2)}) collective-permute-start(bf16[2,128,128]{2,1,0:T(8,128)(2,1)S(1)} %get-tuple-element.332), channel_id=1, source_target_pairs={{0,8},{8,16},{16,24},{24,32},{32,40},{40,48},{48,56},{56,64},{64,7... | collective-permute-start | bytes 196616 | tf_op jit(solution)/shard_map/while/body/eval_jaxpr/ppermute | solution.py:20
  375.6 13.3 %collective-permute-start.1 = (bf16[2,128,128]{2,1,0:T(8,128)(2,1)S(1)}, bf16[2,128,128]{2,1,0:T(8,128)(2,1)S(1)}, u32[]{:S(2)}, u32[]{:S(2)}) collective-permute-start(bf16[2,128,128]{2,1,0:T(8,128)(2,1)S(1)} %get-tuple-element.332), channel_id=1, source_target_pairs={{0,8},{8,16},{16,24},{24,32},{32,40},{40,48},{48,56},{56,64},{64,7... | collective-permute-start | bytes 196616 | tf_op jit(solution)/shard_map/while/body/eval_jaxpr/ppermute | solution.py:20
  389.6 13.3 %collective-permute-start.1 = (bf16[2,128,128]{2,1,0:T(8,128)(2,1)S(1)}, bf16[2,128,128]{2,1,0:T(8,128)(2,1)S(1)}, u32[]{:S(2)}, u32[]{:S(2)}) collective-permute-start(bf16[2,128,128]{2,1,0:T(8,128)(2,1)S(1)} %get-tuple-element.332), channel_id=1, source_target_pairs={{0,8},{8,16},{16,24},{24,32},{32,40},{40,48},{48,56},{56,64},{64,7... | collective-permute-start | bytes 196616 | tf_op jit(solution)/shard_map/while/body/eval_jaxpr/ppermute | solution.py:20
  403.5 13.3 %collective-permute-start.1 = (bf16[2,128,128]{2,1,0:T(8,128)(2,1)S(1)}, bf16[2,128,128]{2,1,0:T(8,128)(2,1)S(1)}, u32[]{:S(2)}, u32[]{:S(2)}) collective-permute-start(bf16[2,128,128]{2,1,0:T(8,128)(2,1)S(1)} %get-tuple-element.332), channel_id=1, source_target_pairs={{0,8},{8,16},{16,24},{24,32},{32,40},{40,48},{48,56},{56,64},{64,7... | collective-permute-start | bytes 196616 | tf_op jit(solution)/shard_map/while/body/eval_jaxpr/ppermute | solution.py:20
  417.5 13.3 %collective-permute-start.1 = (bf16[2,128,128]{2,1,0:T(8,128)(2,1)S(1)}, bf16[2,128,128]{2,1,0:T(8,128)(2,1)S(1)}, u32[]{:S(2)}, u32[]{:S(2)}) collective-permute-start(bf16[2,128,128]{2,1,0:T(8,128)(2,1)S(1)} %get-tuple-element.332), channel_id=1, source_target_pairs={{0,8},{8,16},{16,24},{24,32},{32,40},{40,48},{48,56},{56,64},{64,7... | collective-permute-start | bytes 196616 | tf_op jit(solution)/shard_map/while/body/eval_jaxpr/ppermute | solution.py:20
  431.5 13.3 %collective-permute-start.1 = (bf16[2,128,128]{2,1,0:T(8,128)(2,1)S(1)}, bf16[2,128,128]{2,1,0:T(8,128)(2,1)S(1)}, u32[]{:S(2)}, u32[]{:S(2)}) collective-permute-start(bf16[2,128,128]{2,1,0:T(8,128)(2,1)S(1)} %get-tuple-element.332), channel_id=1, source_target_pairs={{0,8},{8,16},{16,24},{24,32},{32,40},{40,48},{48,56},{56,64},{64,7... | collective-permute-start | bytes 196616 | tf_op jit(solution)/shard_map/while/body/eval_jaxpr/ppermute | solution.py:20
  445.4 13.3 %collective-permute-start.1 = (bf16[2,128,128]{2,1,0:T(8,128)(2,1)S(1)}, bf16[2,128,128]{2,1,0:T(8,128)(2,1)S(1)}, u32[]{:S(2)}, u32[]{:S(2)}) collective-permute-start(bf16[2,128,128]{2,1,0:T(8,128)(2,1)S(1)} %get-tuple-element.332), channel_id=1, source_target_pairs={{0,8},{8,16},{16,24},{24,32},{32,40},{40,48},{48,56},{56,64},{64,7... | collective-permute-start | bytes 196616 | tf_op jit(solution)/shard_map/while/body/eval_jaxpr/ppermute | solution.py:20
  459.4 13.3 %collective-permute-start.1 = (bf16[2,128,128]{2,1,0:T(8,128)(2,1)S(1)}, bf16[2,128,128]{2,1,0:T(8,128)(2,1)S(1)}, u32[]{:S(2)}, u32[]{:S(2)}) collective-permute-start(bf16[2,128,128]{2,1,0:T(8,128)(2,1)S(1)} %get-tuple-element.332), channel_id=1, source_target_pairs={{0,8},{8,16},{16,24},{24,32},{32,40},{40,48},{48,56},{56,64},{64,7... | collective-permute-start | bytes 196616 | tf_op jit(solution)/shard_map/while/body/eval_jaxpr/ppermute | solution.py:20
  473.4 13.3 %collective-permute-start.1 = (bf16[2,128,128]{2,1,0:T(8,128)(2,1)S(1)}, bf16[2,128,128]{2,1,0:T(8,128)(2,1)S(1)}, u32[]{:S(2)}, u32[]{:S(2)}) collective-permute-start(bf16[2,128,128]{2,1,0:T(8,128)(2,1)S(1)} %get-tuple-element.332), channel_id=1, source_target_pairs={{0,8},{8,16},{16,24},{24,32},{32,40},{40,48},{48,56},{56,64},{64,7... | collective-permute-start | bytes 196616 | tf_op jit(solution)/shard_map/while/body/eval_jaxpr/ppermute | solution.py:20
  487.3 13.3 %collective-permute-start.1 = (bf16[2,128,128]{2,1,0:T(8,128)(2,1)S(1)}, bf16[2,128,128]{2,1,0:T(8,128)(2,1)S(1)}, u32[]{:S(2)}, u32[]{:S(2)}) collective-permute-start(bf16[2,128,128]{2,1,0:T(8,128)(2,1)S(1)} %get-tuple-element.332), channel_id=1, source_target_pairs={{0,8},{8,16},{16,24},{24,32},{32,40},{40,48},{48,56},{56,64},{64,7... | collective-permute-start | bytes 196616 | tf_op jit(solution)/shard_map/while/body/eval_jaxpr/ppermute | solution.py:20
  599.0 13.3 %collective-permute-start.1 = (bf16[2,128,128]{2,1,0:T(8,128)(2,1)S(1)}, bf16[2,128,128]{2,1,0:T(8,128)(2,1)S(1)}, u32[]{:S(2)}, u32[]{:S(2)}) collective-permute-start(bf16[2,128,128]{2,1,0:T(8,128)(2,1)S(1)} %get-tuple-element.332), channel_id=1, source_target_pairs={{0,8},{8,16},{16,24},{24,32},{32,40},{40,48},{48,56},{56,64},{64,7... | collective-permute-start | bytes 196616 | tf_op jit(solution)/shard_map/while/body/eval_jaxpr/ppermute | solution.py:20
  613.0 13.3 %collective-permute-start.1 = (bf16[2,128,128]{2,1,0:T(8,128)(2,1)S(1)}, bf16[2,128,128]{2,1,0:T(8,128)(2,1)S(1)}, u32[]{:S(2)}, u32[]{:S(2)}) collective-permute-start(bf16[2,128,128]{2,1,0:T(8,128)(2,1)S(1)} %get-tuple-element.332), channel_id=1, source_target_pairs={{0,8},{8,16},{16,24},{24,32},{32,40},{40,48},{48,56},{56,64},{64,7... | collective-permute-start | bytes 196616 | tf_op jit(solution)/shard_map/while/body/eval_jaxpr/ppermute | solution.py:20
  626.9 13.3 %collective-permute-start.1 = (bf16[2,128,128]{2,1,0:T(8,128)(2,1)S(1)}, bf16[2,128,128]{2,1,0:T(8,128)(2,1)S(1)}, u32[]{:S(2)}, u32[]{:S(2)}) collective-permute-start(bf16[2,128,128]{2,1,0:T(8,128)(2,1)S(1)} %get-tuple-element.332), channel_id=1, source_target_pairs={{0,8},{8,16},{16,24},{24,32},{32,40},{40,48},{48,56},{56,64},{64,7... | collective-permute-start | bytes 196616 | tf_op jit(solution)/shard_map/while/body/eval_jaxpr/ppermute | solution.py:20
  640.9 13.3 %collective-permute-start.1 = (bf16[2,128,128]{2,1,0:T(8,128)(2,1)S(1)}, bf16[2,128,128]{2,1,0:T(8,128)(2,1)S(1)}, u32[]{:S(2)}, u32[]{:S(2)}) collective-permute-start(bf16[2,128,128]{2,1,0:T(8,128)(2,1)S(1)} %get-tuple-element.332), channel_id=1, source_target_pairs={{0,8},{8,16},{16,24},{24,32},{32,40},{40,48},{48,56},{56,64},{64,7... | collective-permute-start | bytes 196616 | tf_op jit(solution)/shard_map/while/body/eval_jaxpr/ppermute | solution.py:20
  654.9 13.3 %collective-permute-start.1 = (bf16[2,128,128]{2,1,0:T(8,128)(2,1)S(1)}, bf16[2,128,128]{2,1,0:T(8,128)(2,1)S(1)}, u32[]{:S(2)}, u32[]{:S(2)}) collective-permute-start(bf16[2,128,128]{2,1,0:T(8,128)(2,1)S(1)} %get-tuple-element.332), channel_id=1, source_target_pairs={{0,8},{8,16},{16,24},{24,32},{32,40},{40,48},{48,56},{56,64},{64,7... | collective-permute-start | bytes 196616 | tf_op jit(solution)/shard_map/while/body/eval_jaxpr/ppermute | solution.py:20
  668.8 13.3 %collective-permute-start.1 = (bf16[2,128,128]{2,1,0:T(8,128)(2,1)S(1)}, bf16[2,128,128]{2,1,0:T(8,128)(2,1)S(1)}, u32[]{:S(2)}, u32[]{:S(2)}) collective-permute-start(bf16[2,128,128]{2,1,0:T(8,128)(2,1)S(1)} %get-tuple-element.332), channel_id=1, source_target_pairs={{0,8},{8,16},{16,24},{24,32},{32,40},{40,48},{48,56},{56,64},{64,7... | collective-permute-start | bytes 196616 | tf_op jit(solution)/shard_map/while/body/eval_jaxpr/ppermute | solution.py:20
  682.8 13.3 %collective-permute-start.1 = (bf16[2,128,128]{2,1,0:T(8,128)(2,1)S(1)}, bf16[2,128,128]{2,1,0:T(8,128)(2,1)S(1)}, u32[]{:S(2)}, u32[]{:S(2)}) collective-permute-start(bf16[2,128,128]{2,1,0:T(8,128)(2,1)S(1)} %get-tuple-element.332), channel_id=1, source_target_pairs={{0,8},{8,16},{16,24},{24,32},{32,40},{40,48},{48,56},{56,64},{64,7... | collective-permute-start | bytes 196616 | tf_op jit(solution)/shard_map/while/body/eval_jaxpr/ppermute | solution.py:20
  696.7 13.3 %collective-permute-start.1 = (bf16[2,128,128]{2,1,0:T(8,128)(2,1)S(1)}, bf16[2,128,128]{2,1,0:T(8,128)(2,1)S(1)}, u32[]{:S(2)}, u32[]{:S(2)}) collective-permute-start(bf16[2,128,128]{2,1,0:T(8,128)(2,1)S(1)} %get-tuple-element.332), channel_id=1, source_target_pairs={{0,8},{8,16},{16,24},{24,32},{32,40},{40,48},{48,56},{56,64},{64,7... | collective-permute-start | bytes 196616 | tf_op jit(solution)/shard_map/while/body/eval_jaxpr/ppermute | solution.py:20
  710.7 13.3 %collective-permute-start.1 = (bf16[2,128,128]{2,1,0:T(8,128)(2,1)S(1)}, bf16[2,128,128]{2,1,0:T(8,128)(2,1)S(1)}, u32[]{:S(2)}, u32[]{:S(2)}) collective-permute-start(bf16[2,128,128]{2,1,0:T(8,128)(2,1)S(1)} %get-tuple-element.332), channel_id=1, source_target_pairs={{0,8},{8,16},{16,24},{24,32},{32,40},{40,48},{48,56},{56,64},{64,7... | collective-permute-start | bytes 196616 | tf_op jit(solution)/shard_map/while/body/eval_jaxpr/ppermute | solution.py:20
  724.7 13.3 %collective-permute-start.1 = (bf16[2,128,128]{2,1,0:T(8,128)(2,1)S(1)}, bf16[2,128,128]{2,1,0:T(8,128)(2,1)S(1)}, u32[]{:S(2)}, u32[]{:S(2)}) collective-permute-start(bf16[2,128,128]{2,1,0:T(8,128)(2,1)S(1)} %get-tuple-element.332), channel_id=1, source_target_pairs={{0,8},{8,16},{16,24},{24,32},{32,40},{40,48},{48,56},{56,64},{64,7... | collective-permute-start | bytes 196616 | tf_op jit(solution)/shard_map/while/body/eval_jaxpr/ppermute | solution.py:20
  738.6 13.3 %collective-permute-start.1 = (bf16[2,128,128]{2,1,0:T(8,128)(2,1)S(1)}, bf16[2,128,128]{2,1,0:T(8,128)(2,1)S(1)}, u32[]{:S(2)}, u32[]{:S(2)}) collective-permute-start(bf16[2,128,128]{2,1,0:T(8,128)(2,1)S(1)} %get-tuple-element.332), channel_id=1, source_target_pairs={{0,8},{8,16},{16,24},{24,32},{32,40},{40,48},{48,56},{56,64},{64,7... | collective-permute-start | bytes 196616 | tf_op jit(solution)/shard_map/while/body/eval_jaxpr/ppermute | solution.py:20
  752.6 13.3 %collective-permute-start.1 = (bf16[2,128,128]{2,1,0:T(8,128)(2,1)S(1)}, bf16[2,128,128]{2,1,0:T(8,128)(2,1)S(1)}, u32[]{:S(2)}, u32[]{:S(2)}) collective-permute-start(bf16[2,128,128]{2,1,0:T(8,128)(2,1)S(1)} %get-tuple-element.332), channel_id=1, source_target_pairs={{0,8},{8,16},{16,24},{24,32},{32,40},{40,48},{48,56},{56,64},{64,7... | collective-permute-start | bytes 196616 | tf_op jit(solution)/shard_map/while/body/eval_jaxpr/ppermute | solution.py:20
  864.3 13.3 %collective-permute-start.1 = (bf16[2,128,128]{2,1,0:T(8,128)(2,1)S(1)}, bf16[2,128,128]{2,1,0:T(8,128)(2,1)S(1)}, u32[]{:S(2)}, u32[]{:S(2)}) collective-permute-start(bf16[2,128,128]{2,1,0:T(8,128)(2,1)S(1)} %get-tuple-element.332), channel_id=1, source_target_pairs={{0,8},{8,16},{16,24},{24,32},{32,40},{40,48},{48,56},{56,64},{64,7... | collective-permute-start | bytes 196616 | tf_op jit(solution)/shard_map/while/body/eval_jaxpr/ppermute | solution.py:20
  878.2 13.3 %collective-permute-start.1 = (bf16[2,128,128]{2,1,0:T(8,128)(2,1)S(1)}, bf16[2,128,128]{2,1,0:T(8,128)(2,1)S(1)}, u32[]{:S(2)}, u32[]{:S(2)}) collective-permute-start(bf16[2,128,128]{2,1,0:T(8,128)(2,1)S(1)} %get-tuple-element.332), channel_id=1, source_target_pairs={{0,8},{8,16},{16,24},{24,32},{32,40},{40,48},{48,56},{56,64},{64,7... | collective-permute-start | bytes 196616 | tf_op jit(solution)/shard_map/while/body/eval_jaxpr/ppermute | solution.py:20
  892.2 13.3 %collective-permute-start.1 = (bf16[2,128,128]{2,1,0:T(8,128)(2,1)S(1)}, bf16[2,128,128]{2,1,0:T(8,128)(2,1)S(1)}, u32[]{:S(2)}, u32[]{:S(2)}) collective-permute-start(bf16[2,128,128]{2,1,0:T(8,128)(2,1)S(1)} %get-tuple-element.332), channel_id=1, source_target_pairs={{0,8},{8,16},{16,24},{24,32},{32,40},{40,48},{48,56},{56,64},{64,7... | collective-permute-start | bytes 196616 | tf_op jit(solution)/shard_map/while/body/eval_jaxpr/ppermute | solution.py:20
  906.2 13.3 %collective-permute-start.1 = (bf16[2,128,128]{2,1,0:T(8,128)(2,1)S(1)}, bf16[2,128,128]{2,1,0:T(8,128)(2,1)S(1)}, u32[]{:S(2)}, u32[]{:S(2)}) collective-permute-start(bf16[2,128,128]{2,1,0:T(8,128)(2,1)S(1)} %get-tuple-element.332), channel_id=1, source_target_pairs={{0,8},{8,16},{16,24},{24,32},{32,40},{40,48},{48,56},{56,64},{64,7... | collective-permute-start | bytes 196616 | tf_op jit(solution)/shard_map/while/body/eval_jaxpr/ppermute | solution.py:20
  920.1 13.3 %collective-permute-start.1 = (bf16[2,128,128]{2,1,0:T(8,128)(2,1)S(1)}, bf16[2,128,128]{2,1,0:T(8,128)(2,1)S(1)}, u32[]{:S(2)}, u32[]{:S(2)}) collective-permute-start(bf16[2,128,128]{2,1,0:T(8,128)(2,1)S(1)} %get-tuple-element.332), channel_id=1, source_target_pairs={{0,8},{8,16},{16,24},{24,32},{32,40},{40,48},{48,56},{56,64},{64,7... | collective-permute-start | bytes 196616 | tf_op jit(solution)/shard_map/while/body/eval_jaxpr/ppermute | solution.py:20
  934.1 13.3 %collective-permute-start.1 = (bf16[2,128,128]{2,1,0:T(8,128)(2,1)S(1)}, bf16[2,128,128]{2,1,0:T(8,128)(2,1)S(1)}, u32[]{:S(2)}, u32[]{:S(2)}) collective-permute-start(bf16[2,128,128]{2,1,0:T(8,128)(2,1)S(1)} %get-tuple-element.332), channel_id=1, source_target_pairs={{0,8},{8,16},{16,24},{24,32},{32,40},{40,48},{48,56},{56,64},{64,7... | collective-permute-start | bytes 196616 | tf_op jit(solution)/shard_map/while/body/eval_jaxpr/ppermute | solution.py:20
  948.0 13.3 %collective-permute-start.1 = (bf16[2,128,128]{2,1,0:T(8,128)(2,1)S(1)}, bf16[2,128,128]{2,1,0:T(8,128)(2,1)S(1)}, u32[]{:S(2)}, u32[]{:S(2)}) collective-permute-start(bf16[2,128,128]{2,1,0:T(8,128)(2,1)S(1)} %get-tuple-element.332), channel_id=1, source_target_pairs={{0,8},{8,16},{16,24},{24,32},{32,40},{40,48},{48,56},{56,64},{64,7... | collective-permute-start | bytes 196616 | tf_op jit(solution)/shard_map/while/body/eval_jaxpr/ppermute | solution.py:20
  962.0 13.3 %collective-permute-start.1 = (bf16[2,128,128]{2,1,0:T(8,128)(2,1)S(1)}, bf16[2,128,128]{2,1,0:T(8,128)(2,1)S(1)}, u32[]{:S(2)}, u32[]{:S(2)}) collective-permute-start(bf16[2,128,128]{2,1,0:T(8,128)(2,1)S(1)} %get-tuple-element.332), channel_id=1, source_target_pairs={{0,8},{8,16},{16,24},{24,32},{32,40},{40,48},{48,56},{56,64},{64,7... | collective-permute-start | bytes 196616 | tf_op jit(solution)/shard_map/while/body/eval_jaxpr/ppermute | solution.py:20
  976.0 13.3 %collective-permute-start.1 = (bf16[2,128,128]{2,1,0:T(8,128)(2,1)S(1)}, bf16[2,128,128]{2,1,0:T(8,128)(2,1)S(1)}, u32[]{:S(2)}, u32[]{:S(2)}) collective-permute-start(bf16[2,128,128]{2,1,0:T(8,128)(2,1)S(1)} %get-tuple-element.332), channel_id=1, source_target_pairs={{0,8},{8,16},{16,24},{24,32},{32,40},{40,48},{48,56},{56,64},{64,7... | collective-permute-start | bytes 196616 | tf_op jit(solution)/shard_map/while/body/eval_jaxpr/ppermute | solution.py:20
  989.9 13.3 %collective-permute-start.1 = (bf16[2,128,128]{2,1,0:T(8,128)(2,1)S(1)}, bf16[2,128,128]{2,1,0:T(8,128)(2,1)S(1)}, u32[]{:S(2)}, u32[]{:S(2)}) collective-permute-start(bf16[2,128,128]{2,1,0:T(8,128)(2,1)S(1)} %get-tuple-element.332), channel_id=1, source_target_pairs={{0,8},{8,16},{16,24},{24,32},{32,40},{40,48},{48,56},{56,64},{64,7... | collective-permute-start | bytes 196616 | tf_op jit(solution)/shard_map/while/body/eval_jaxpr/ppermute | solution.py:20
  1003.9 13.3 %collective-permute-start.1 = (bf16[2,128,128]{2,1,0:T(8,128)(2,1)S(1)}, bf16[2,128,128]{2,1,0:T(8,128)(2,1)S(1)}, u32[]{:S(2)}, u32[]{:S(2)}) collective-permute-start(bf16[2,128,128]{2,1,0:T(8,128)(2,1)S(1)} %get-tuple-element.332), channel_id=1, source_target_pairs={{0,8},{8,16},{16,24},{24,32},{32,40},{40,48},{48,56},{56,64},{64,7... | collective-permute-start | bytes 196616 | tf_op jit(solution)/shard_map/while/body/eval_jaxpr/ppermute | solution.py:20
  (86 other events, 2532.0 us)
Sparse Core Ops, SparseCore 0:
  9.4 69.9 all-gather.1
